TPU v7x, 256 devices: a whole 4x4x8 slice. The times are simulated.
256 devices in a mesh: row: 8 (over z), col: 32 (over y, x, core).
Axes of the slice: x: 4, y: 4, z: 8, core: 2. Of those that a mesh axis runs over, the one named last changes fastest.
Arguments:
- embeds: bfloat16 [24576, 768], P('col'), may hold values from -6 to 6
- labels: bfloat16 [24576, 1000], P('col'), may hold values from -6 to 6
- sharpness: float32 [24576], P('col'), may hold values from 0.5 to 100
- pattern: int32 [192, 16], P('col'), may hold values from 0 to 191, as said below
- mask_pos: int32 [24576, 50], P('col'), may hold values from 0 to 2047, as said below
Outputs:
- propagated: bfloat16 [24576, 1000], P('col', 'row')
Inputs may be any that keep to these rules, and one draw needn't show every extreme that they name: `pattern`: split the row blocks into runs of 6 and the slots into runs of 2; within one run of row blocks and one run of slots, ids that lie in the same run of 6 block ids are equal. `mask_pos`: the 50 positions of a row are distinct; position k * 128 + m names row m of the row block's k-th candidate block.
All inputs are finite; a program needn't handle non-finite values.
Results may differ from a plain program's by a relative error of at most 0.012.
Values may be sent and summed in bfloat16 or wider, within the bound.
No kernel may reach another device: no remote copies, remote signals or barrier semaphores. Data moves between devices by JAX's collectives and lax.ppermute only.
A program may use at most 128 MiB of HBM per device.

v0:
```python
import math
import jax
import jax.numpy as jnp
from jax import lax
from jax.sharding import PartitionSpec as P

BLOCK = 128
SLOTS = 16
mixing = 0.75
lowest_logit = -1e30
COL = ("chip", "core")


def gather_columns(x):
    rows_here, width = x.shape
    same_core = lax.all_gather(x, "chip", tiled=True).reshape(-1, BLOCK, width)
    other_core = lax.ppermute(same_core, "core", [(0, 1), (1, 0)])
    return (same_core, other_core)


def body(embeds, labels, sharpness, pattern, mask_pos):
    rows_here, width = embeds.shape
    classes = labels.shape[1]
    n_col = lax.axis_size(COL)
    n_row = lax.axis_size("row")
    row_pos = lax.axis_index("row")
    blocks_here = rows_here // BLOCK
    slots_here = SLOTS // n_row
    span = slots_here * BLOCK
    per_device = classes // n_row
    owners = pattern // blocks_here
    local_ids = pattern % blocks_here
    my_owners = lax.dynamic_slice_in_dim(owners, row_pos * slots_here, slots_here, 1)
    my_ids = lax.dynamic_slice_in_dim(local_ids, row_pos * slots_here, slots_here, 1)
    peers = jnp.arange(n_col, dtype=jnp.int32)
    wanted = jnp.max(jnp.where(my_owners[..., None] == peers, my_ids[..., None], 0), axis=(0, 1))
    requested = lax.all_to_all(wanted, COL, split_axis=0, concat_axis=0, tiled=True)
    embedding_tiles = embeds.reshape(blocks_here, BLOCK, width)
    send_emb = embedding_tiles[requested]
    my_labels = lax.dynamic_slice_in_dim(labels, row_pos * per_device, per_device, 1)
    lanes = -(-per_device // 128) * 128
    my_labels = jnp.pad(my_labels, ((0, 0), (0, lanes - per_device)))
    all_labels = gather_columns(my_labels)
    shifted = mask_pos - row_pos * span
    shifted = jnp.where((shifted >= 0) & (shifted < span), shifted, span)
    positions = jnp.arange(span, dtype=jnp.int32)
    in_mask = jnp.any(shifted[:, :, None] == positions[None, None, :], axis=1)
    in_mask = in_mask.reshape(blocks_here, BLOCK, span)
    fetched_emb = lax.all_to_all(send_emb, COL, split_axis=0, concat_axis=0, tiled=True)
    candidate_ids = fetched_emb[my_owners].reshape(blocks_here, span, width)
    scores = jnp.einsum(
        "evg,erg->evr", embedding_tiles, candidate_ids, preferred_element_type=jnp.float32
    ) / math.sqrt(width)
    logits = scores * sharpness.reshape(blocks_here, BLOCK, 1)
    local_max = jnp.max(jnp.where(in_mask, logits, lowest_logit), axis=2)
    local_sum = jnp.sum(jnp.where(in_mask, jnp.exp(logits - local_max[..., None]), 0.0), axis=2)
    local_weights = jnp.where(in_mask, jnp.exp(logits - local_max[..., None]), 0.0).astype(
        jnp.bfloat16
    )
    stats = lax.all_gather(jnp.stack([local_max, local_sum]), "row")
    all_weights = lax.all_gather(local_weights, "row")
    top = jnp.max(stats[:, 0], axis=0)
    totals = jnp.sum(stats[:, 1] * jnp.exp(stats[:, 0] - top), axis=0)
    factors = jnp.exp(stats[:, 0] - top) / totals
    shard_of = pattern // blocks_here
    on_this_core = (shard_of % 2 == lax.axis_index("core"))[..., None, None]
    pair_ids = shard_of // 2 * blocks_here + pattern % blocks_here

    def propagate_using(gathered, seed, whole=False):
        if whole:
            candidates = gathered[pattern]
        else:
            same_core, other_core = gathered
            candidates = jnp.where(on_this_core, same_core[pair_ids], other_core[pair_ids])
        candidates = candidates.reshape(blocks_here, n_row, span, lanes)
        pieces = jnp.einsum(
            "gtmk,tgkc->gtmc", all_weights, candidates, preferred_element_type=jnp.float32
        )
        pieces = (pieces * factors[..., None]).astype(jnp.bfloat16)
        summed = jnp.sum(pieces.astype(jnp.float32), axis=0).reshape(rows_here, lanes)
        return (mixing * summed + (1.0 - mixing) * seed.astype(jnp.float32)).astype(jnp.bfloat16)

    spread = propagate_using(all_labels, my_labels)
    whole_spread = lax.all_gather(spread, COL, tiled=True).reshape(-1, BLOCK, lanes)
    return propagate_using(whole_spread, my_labels, whole=True)[:, :per_device]


def solution(mesh):
    devices = mesh.devices
    fine = jax.sharding.Mesh(
        devices.reshape(devices.shape[0], devices.shape[1] // 2, 2), ("row", "chip", "core")
    )
    placed = (P(COL, None), P(COL, None), P(COL), P(COL, None), P(COL, None))
    return jax.shard_map(body, mesh=fine, in_specs=placed, out_specs=P(COL, "row"), check_vma=False)
```

profile of v0, /device:TPU:1, one launch (start us, length us, event | category | flops | bytes accessed | tf_op | source)
XLA Modules:
  0.0 252.2 jit_solution(4640348290725915735)
XLA Ops:
  6.5 0.8 fusion.23
  7.4 0.7 compare_select_fusion.1
  8.3 15.3 %all_to_all.17 = s32[32,1,1]{2,1,0:T(1,128)S(1)} all-to-all(s32[32,1,1]{2,1,0:T(1,128)S(1)} %copy.42), channel_id=1, replica_groups=mesh['row'=8,'chip'=16,'core'=2] {'chip','core'}, dimensions={0} | all-to-all | bytes 256 | tf_op jit(solution)/shard_map/all_to_all | solution.py:37
  23.7 0.7 reduce.1
  24.4 4.9 %gather_fusion = bf16[32,128,768]{2,1,0:T(8,128)(2,1)} fusion(bf16[6,128,768]{2,1,0:T(8,128)(2,1)} %bitcast.49, s32[1024]{0:T(1024)S(1)} %pad_clamp_fusion.3), kind=kCustom, calls=%fused_computation | custom fusion | bytes 12583040 | tf_op jit(solution)/shard_map/gather | solution.py:39
  29.2 5.3 %all-to-all-start.1 = ((bf16[32,128,768]{2,1,0:T(8,128)(2,1)}), bf16[32,128,768]{2,1,0:T(8,128)(2,1)}, u32[]{:S(2)}, u32[]{:S(2)}) async-start(bf16[32,128,768]{2,1,0:T(8,128)(2,1)} %gather_fusion), calls=%async_computation.1 | async-start | bytes 12582912 | tf_op jit(solution)/shard_map/all_to_all | solution.py:49
  34.8 0.7 pad.4
  35.7 7.2 %fusion = pred[768,256]{1,0:T(8,128)(4,1)S(1)} fusion(s32[768,50]{0,1:T(8,128)S(1)} %and_select_fusion), kind=kLoop, calls=%fused_computation.6 | loop fusion | flops 19464192 | bytes 350208 | tf_op jit(solution)/shard_map/reduce_or | solution.py:47
  43.3 68.2 %all-to-all-done.1 = bf16[32,128,768]{2,1,0:T(8,128)(2,1)} async-done(((bf16[32,128,768]{2,1,0:T(8,128)(2,1)}), bf16[32,128,768]{2,1,0:T(8,128)(2,1)}, u32[]{:S(2)}, u32[]{:S(2)}) %all-to-all-start.1) | async-done | bytes 6291488 | tf_op jit(solution)/shard_map/all_to_all | solution.py:49
  111.5 5.2 %gather_fusion.1 = bf16[12,128,768]{2,1,0:T(8,128)(2,1)} fusion(bf16[32,128,768]{2,1,0:T(8,128)(2,1)} %all-to-all-done.1, s32[1024]{0:T(1024)S(1)} %pad_clamp_fusion.2), kind=kCustom, calls=%fused_computation.1 | custom fusion | bytes 4718640 | tf_op jit(solution)/shard_map/gather | solution.py:50
  116.8 2.5 select_reduce_fusion
  119.5 1.0 copy.45
  120.5 8.6 %all-gather.6.cloned.1.call-done = bf16[12288,128]{1,0:T(8,128)(2,1)} async-done(((bf16[768,128]{1,0:T(8,128)(2,1)}), bf16[12288,128]{1,0:T(8,128)(2,1)}) %all-gather.6.cloned.1.call-update) | async-done | bytes 3145744 | tf_op jit(solution)/shard_map/all_gather | solution.py:16
  129.1 1.3 collective-permute-start
  130.6 4.6 %gather_fusion.2 = bf16[96,128,128]{2,1,0:T(8,128)(2,1)} fusion(bf16[96,128,128]{2,1,0:T(8,128)(2,1)} %bitcast.52, s32[1024]{0:T(1024)S(1)} %pad_clamp_fusion.1), kind=kCustom, calls=%fused_computation.2 | custom fusion | bytes 6291840 | tf_op jit(solution)/shard_map/gather | solution.py:74
  135.2 22.3 %all-gather.1 = f32[16,6,128]{2,1,0:T(8,128)S(1)} all-gather(f32[2,6,128]{2,1,0:T(8,128)S(1)} %pad_maximum_fusion), channel_id=3, replica_groups=mesh['row'=8,'chip'=16,'core'=2] {'row'}, dimensions={0}, use_global_device_ids=true | all-gather | bytes 55296 | tf_op jit(solution)/shard_map/all_gather | solution.py:60
  157.6 4.7 %gather_fusion.3 = bf16[96,128,128]{2,1,0:T(8,128)(2,1)} fusion(bf16[96,128,128]{2,1,0:T(8,128)(2,1)} %collective-permute-done, s32[1024]{0:T(1024)S(1)} %pad_clamp_fusion.1), kind=kCustom, calls=%fused_computation.3 | custom fusion | bytes 6291840 | tf_op jit(solution)/shard_map/gather | solution.py:74
  162.3 13.1 %all-gather.10.cloned.1.call-done = bf16[48,128,256]{2,1,0:T(8,128)(2,1)} async-done(((bf16[6,128,256]{2,1,0:T(8,128)(2,1)}), bf16[48,128,256]{2,1,0:T(8,128)(2,1)}) %all-gather.10.cloned.1.call-update) | async-done | bytes 3145744 | tf_op jit(solution)/shard_map/all_gather | solution.py:61
  175.4 5.9 %convert_reduce_fusion.1 = f32[6,128,128]{2,1,0:T(8,128)S(1)} fusion(f32[8,6,128]{2,1,0:T(8,128)S(1)} %fusion.21, bf16[8,6,128,256]{3,2,1,0:T(8,128)(2,1)} %bitcast.66, bf16[6,8,256,128]{3,2,1,0:T(8,128)(2,1)} %bitcast.53, bf16[6,8,256,128]{3,2,1,0:T(8,128)(2,1)} %bitcast.54, pred[6,8,256]{2,1,0:T(8,128)(4,1)S(1)} %broadcast_in_dim.64), kind=kOutput, calls=%fused_computation.13 | convolution fusion | flops 407273472 | bytes 9867264 | tf_op jit(solution)/shard_map/gtmk,tgkc->gtmc/dot_general | solution.py:76
  181.3 0.8 fusion.17
  182.2 53.4 %all-gather.8.cloned.1.call-done = bf16[24576,128]{1,0:T(8,128)(2,1)} async-done(((bf16[768,128]{1,0:T(8,128)(2,1)}), bf16[24576,128]{1,0:T(8,128)(2,1)}) %all-gather.8.cloned.1.call-update) | async-done | bytes 6291472 | tf_op jit(solution)/shard_map/all_gather | solution.py:84
  235.5 5.5 %gather_fusion.4 = bf16[96,128,128]{2,1,0:T(8,128)(2,1)} fusion(bf16[192,128,128]{2,1,0:T(8,128)(2,1)} %bitcast.58, s32[1024]{0:T(1024)S(1)} %pad_clamp_fusion), kind=kCustom, calls=%fused_computation.4 | custom fusion | bytes 6291840 | tf_op jit(solution)/shard_map/gather | solution.py:71
  241.0 3.9 %convert_reduce_fusion = f32[6,128,128]{2,1,0:T(8,128)S(1)} fusion(f32[8,6,128]{2,1,0:T(8,128)S(1)} %fusion.21, bf16[8,6,128,256]{3,2,1,0:T(8,128)(2,1)} %bitcast.67, bf16[6,8,256,128]{3,2,1,0:T(8,128)(2,1)} %bitcast.55), kind=kOutput, calls=%fused_computation.11 | convolution fusion | flops 405700608 | bytes 6709248 | tf_op jit(solution)/shard_map/gtmk,tgkc->gtmc/dot_general | solution.py:76
  244.9 0.7 fusion.16
  (40 shorter events, 1.7 us)
Async XLA Ops:
  6.5 28.0 %copy-start = (bf16[768,1000]{0,1:T(8,128)(2,1)S(1)}, bf16[768,1000]{0,1:T(8,128)(2,1)}, u32[]{:S(2)}) copy-start(bf16[768,1000]{0,1:T(8,128)(2,1)} %param.6) | copy-start | bytes 4608004
  29.2 6.4 %copy-start.2 = (s32[768,50]{0,1:T(8,128)S(1)}, s32[768,50]{0,1:T(8,128)}, u32[]{:S(2)}) copy-start(s32[768,50]{0,1:T(8,128)} %param.9) | copy-start | bytes 460804
  29.2 14.0 %copy-start.3 = (f32[768]{0:T(1024)S(1)}, f32[768]{0:T(1024)}, u32[]{:S(2)}) copy-start(f32[768]{0:T(1024)} %param.7) | copy-start | bytes 9220
  29.2 82.3 %all-to-all-start.1 = ((bf16[32,128,768]{2,1,0:T(8,128)(2,1)}), bf16[32,128,768]{2,1,0:T(8,128)(2,1)}, u32[]{:S(2)}, u32[]{:S(2)}) async-start(bf16[32,128,768]{2,1,0:T(8,128)(2,1)} %gather_fusion), calls=%async_computation.1 | async-start | bytes 12582912 | tf_op jit(solution)/shard_map/all_to_all | solution.py:49
  34.5 94.6 %all-gather.6.cloned.1.call-start = ((), (), s32[]{:S(2)}) async-start(), calls=%async_computation.2 | async-start | bytes 3342336 | tf_op jit(solution)/shard_map/all_gather | solution.py:16
  34.8 82.0 %copy-start.1 = (bf16[768,768]{1,0:T(8,128)(2,1)S(1)}, bf16[768,768]{1,0:T(8,128)(2,1)}, u32[]{:S(2)}) copy-start(bf16[768,768]{1,0:T(8,128)(2,1)} %param.5) | copy-start | bytes 3538948
  35.6 139.8 %all-gather.10.cloned.1.call-start = ((), (), s32[]{:S(2)}) async-start(), calls=%async_computation.4 | async-start | bytes 3538944 | tf_op jit(solution)/shard_map/all_gather | solution.py:61
  120.5 115.1 %all-gather.8.cloned.1.call-start = ((), (), s32[]{:S(2)}) async-start(), calls=%async_computation.3 | async-start | bytes 6488064 | tf_op jit(solution)/shard_map/all_gather | solution.py:84
  129.1 28.5 %collective-permute-start = (bf16[96,128,128]{2,1,0:T(8,128)(2,1)}, bf16[96,128,128]{2,1,0:T(8,128)(2,1)}, u32[]{:S(2)}, u32[]{:S(2)}) collective-permute-start(bf16[96,128,128]{2,1,0:T(8,128)(2,1)} %bitcast.51), channel_id=1, source_target_pairs={{0,1},{1,0},{2,3},{3,2},{4,5},{5,4},{6,7},{7,6},{8,9},{9,8},{10,11... | collective-permute-start | bytes 9437192 | tf_op jit(solution)/shard_map/ppermute | solution.py:17
Sparse Core Ops, SparseCore 0:
  37.7 91.3 all-gather.5
  130.9 44.4 all-gather.9
  182.2 53.3 all-gather.7
where the time goes:
time: 253 us; the launch traced here: 252 us
  waiting for transfers between devices  143 us (57%)
  blocking collectives  37.7 us (15%)
  local copies, waits for them, and re-layouts  27.4 us (11%)
  between operations  13.3 us (5%)
  matrix products  12.2 us (5%)
  other arithmetic  11.5 us (5%)
  starting transfers between devices  6.68 us (3%)
    all_to_all x1, waiting for transfers between devices, body(): lax.all_to_all(send_emb, COL, split_axis=0, concat_axis=0, tiled=True)  68.2 us
    all_gather x1, waiting for transfers between devices, body(): lax.all_gather(spread, COL, tiled=True).reshape(-1, BLOCK, lanes)  53.4 us
    all_gather x1, blocking collectives, body(): stats = lax.all_gather(jnp.stack([local_max, local_sum]), 'row')  22.3 us
    all_to_all x1, blocking collectives, body(): lax.all_to_all(wanted, COL, split_axis=0, concat_axis=0, tiled=True)  15.3 us
    all_gather x1, waiting for transfers between devices, body(): all_weights = lax.all_gather(local_weights, 'row')  13.1 us
    dot_general x2, matrix products, propagate_using(): jnp.einsum('gtmk,tgkc->gtmc', all_weights, candidates, preferred_element_...  9.73 us
    all_gather x1, waiting for transfers between devices, gather_columns(): same_core = lax.all_gather(x, 'chip', tiled=True).reshape(-1, BLOCK, width)  8.61 us
    reduce_or x1, other arithmetic, body(): in_mask = jnp.any(shifted[:, :, None] == positions[None, None, :], axis=1)  7.22 us
  transfers between devices with their start and end apart: 5, of which 4 were waited for; matrix products, arithmetic and copies ran while one was open for 11% of the time, Pallas kernels for 0%

commit v1 on v0

--- a/solution.py
+++ b/solution.py
@@ -3,6 +3,7 @@
 import jax.numpy as jnp
 from jax import lax
 from jax.sharding import PartitionSpec as P
+from jax.lax import all_to_all, axis_size
 
 BLOCK = 128
 SLOTS = 16
@@ -13,7 +14,10 @@
 
 def gather_columns(x):
     rows_here, width = x.shape
-    same_core = lax.all_gather(x, "chip", tiled=True).reshape(-1, BLOCK, width)
+    write_bench_on = lambda local_x: jnp.concatenate(
+        all_to_all(jnp.stack([local_x] * axis_size("chip")), "chip", 0, 0), 0
+    )
+    same_core = write_bench_on(x).reshape(-1, BLOCK, width)
     other_core = lax.ppermute(same_core, "core", [(0, 1), (1, 0)])
     return (same_core, other_core)
 

time: 253 us -> 276 us (1.091)
  waiting for transfers between devices: 143 us -> 156 us
  starting transfers between devices: 6.68 us -> 16 us
    all_to_all x0 -> x1, waiting for transfers between devices: none -> 26.3 us  [gather_columns(): all_to_all(jnp.stack([local_x] * axis_size('chip')), 'chip', 0, 0)]
    all_gather x1, waiting for transfers between devices: 13.1 us -> 0.02 us  [body(): all_weights = lax.all_gather(local_weights, 'row')]
    all_gather x1 -> x0, waiting for transfers between devices: 8.61 us -> none  [gather_columns(): same_core = lax.all_gather(x, 'chip', tiled=True).reshape(-1, BLOCK, width)]
    all_to_all x0 -> x1, starting transfers between devices: none -> 7.32 us  [gather_columns(): all_to_all(jnp.stack([local_x] * axis_size('chip')), 'chip', 0, 0)]
    all_to_all x1, waiting for transfers between devices: 68.2 us -> 73 us  [body(): lax.all_to_all(send_emb, COL, split_axis=0, concat_axis=0, tiled=True)]
  transfers between devices with their start and end apart: 5 -> 5, of which waited for: 4 -> 4; matrix products, arithmetic and copies ran while one was open for 11% -> 9% of each run, Pallas kernels for 0% -> 0%
where the time goes in v1:
time: 276 us
  waiting for transfers between devices  156 us (57%)
  blocking collectives  37.8 us (14%)
  local copies, waits for them, and re-layouts  28.8 us (10%)
  starting transfers between devices  16 us (6%)
  between operations  13.6 us (5%)
  matrix products  12.2 us (4%)
  other arithmetic  11.5 us (4%)
    all_to_all x1, waiting for transfers between devices, body(): lax.all_to_all(send_emb, COL, split_axis=0, concat_axis=0, tiled=True)  73 us
    all_gather x1, waiting for transfers between devices, body(): lax.all_gather(spread, COL, tiled=True).reshape(-1, BLOCK, lanes)  55.9 us
    all_to_all x1, waiting for transfers between devices, gather_columns(): all_to_all(jnp.stack([local_x] * axis_size('chip')), 'chip', 0, 0)  26.3 us
    all_gather x1, blocking collectives, body(): stats = lax.all_gather(jnp.stack([local_max, local_sum]), 'row')  22.4 us
    all_to_all x1, blocking collectives, body(): lax.all_to_all(wanted, COL, split_axis=0, concat_axis=0, tiled=True)  15.3 us
    dot_general x2, matrix products, propagate_using(): jnp.einsum('gtmk,tgkc->gtmc', all_weights, candidates, preferred_element_...  9.74 us
    all_to_all x1, starting transfers between devices, gather_columns(): all_to_all(jnp.stack([local_x] * axis_size('chip')), 'chip', 0, 0)  7.32 us
    reduce_or x1, other arithmetic, body(): in_mask = jnp.any(shifted[:, :, None] == positions[None, None, :], axis=1)  7.22 us
  transfers between devices with their start and end apart: 5, of which 4 were waited for; matrix products, arithmetic and copies ran while one was open for 9% of the time, Pallas kernels for 0%

profile of v1, /device:TPU:1, one launch (start us, length us, event | category | flops | bytes accessed | tf_op | source)
XLA Modules:
  0.0 275.9 jit_solution(18244483634525050729)
XLA Ops:
  6.5 0.8 fusion.23
  7.4 0.7 compare_select_fusion.1
  8.3 15.3 %all_to_all.22 = s32[32,1,1]{2,1,0:T(1,128)S(1)} all-to-all(s32[32,1,1]{2,1,0:T(1,128)S(1)} %copy.42), channel_id=1, replica_groups=mesh['row'=8,'chip'=16,'core'=2] {'chip','core'}, dimensions={0} | all-to-all | bytes 256 | tf_op jit(solution)/shard_map/all_to_all | solution.py:41
  24.4 4.9 %gather_fusion = bf16[32,128,768]{2,1,0:T(8,128)(2,1)} fusion(bf16[6,128,768]{2,1,0:T(8,128)(2,1)} %bitcast.49, s32[1024]{0:T(1024)S(1)} %pad_clamp_fusion.3), kind=kCustom, calls=%fused_computation | custom fusion | bytes 12583040 | tf_op jit(solution)/shard_map/gather | solution.py:43
  29.2 5.3 %all-to-all-start.1 = ((bf16[32,128,768]{2,1,0:T(8,128)(2,1)}), bf16[32,128,768]{2,1,0:T(8,128)(2,1)}, u32[]{:S(2)}, u32[]{:S(2)}) async-start(bf16[32,128,768]{2,1,0:T(8,128)(2,1)} %gather_fusion), calls=%async_computation.1 | async-start | bytes 12582912 | tf_op jit(solution)/shard_map/all_to_all | solution.py:53
  34.9 73.0 %all-to-all-done.1 = bf16[32,128,768]{2,1,0:T(8,128)(2,1)} async-done(((bf16[32,128,768]{2,1,0:T(8,128)(2,1)}), bf16[32,128,768]{2,1,0:T(8,128)(2,1)}, u32[]{:S(2)}, u32[]{:S(2)}) %all-to-all-start.1) | async-done | bytes 6291488 | tf_op jit(solution)/shard_map/all_to_all | solution.py:53
  107.8 2.3 stack.8
  110.1 7.3 %all-to-all-start.2 = ((bf16[16,768,128]{2,1,0:T(8,128)(2,1)}), bf16[16,768,128]{2,1,0:T(8,128)(2,1)}, u32[]{:S(2)}, u32[]{:S(2)}) async-start(bf16[16,768,128]{2,1,0:T(8,128)(2,1)} %stack.8), calls=%async_computation.2 | async-start | bytes 6291456 | tf_op jit(solution)/shard_map/all_to_all | solution.py:18
  117.5 7.2 %fusion = pred[768,256]{1,0:T(8,128)(4,1)S(1)} fusion(s32[768,50]{0,1:T(8,128)S(1)} %and_select_fusion), kind=kLoop, calls=%fused_computation.6 | loop fusion | flops 19464192 | bytes 350208 | tf_op jit(solution)/shard_map/reduce_or | solution.py:51
  125.1 5.0 %gather_fusion.1 = bf16[12,128,768]{2,1,0:T(8,128)(2,1)} fusion(bf16[32,128,768]{2,1,0:T(8,128)(2,1)} %all-to-all-done.1, s32[1024]{0:T(1024)S(1)} %pad_clamp_fusion.2), kind=kCustom, calls=%fused_computation.1 | custom fusion | bytes 4718640 | tf_op jit(solution)/shard_map/gather | solution.py:54
  130.1 2.5 select_reduce_fusion
  132.8 1.0 copy.45
  133.8 26.3 %all-to-all-done.2 = bf16[16,768,128]{2,1,0:T(8,128)(2,1)} async-done(((bf16[16,768,128]{2,1,0:T(8,128)(2,1)}), bf16[16,768,128]{2,1,0:T(8,128)(2,1)}, u32[]{:S(2)}, u32[]{:S(2)}) %all-to-all-start.2) | async-done | bytes 3145760 | tf_op jit(solution)/shard_map/all_to_all | solution.py:18
  160.2 3.3 %collective-permute-start = (bf16[96,128,128]{2,1,0:T(8,128)(2,1)}, bf16[96,128,128]{2,1,0:T(8,128)(2,1)}, u32[]{:S(2)}, u32[]{:S(2)}) collective-permute-start(bf16[96,128,128]{2,1,0:T(8,128)(2,1)} %bitcast.8), channel_id=1, source_target_pairs={{0,1},{1,0},{2,3},{3,2},{4,5},{5,4},{6,7},{7,6},{8,9},{9,8},{10,11... | collective-permute-start | bytes 9437192 | tf_op jit(solution)/shard_map/ppermute | solution.py:21
  163.7 4.6 %gather_fusion.2 = bf16[96,128,128]{2,1,0:T(8,128)(2,1)} fusion(bf16[96,128,128]{2,1,0:T(8,128)(2,1)} %bitcast.8, s32[1024]{0:T(1024)S(1)} %pad_clamp_fusion.1), kind=kCustom, calls=%fused_computation.2 | custom fusion | bytes 6291840 | tf_op jit(solution)/shard_map/gather | solution.py:78
  168.3 0.8 collective-permute-done
  169.1 4.6 %gather_fusion.3 = bf16[96,128,128]{2,1,0:T(8,128)(2,1)} fusion(bf16[96,128,128]{2,1,0:T(8,128)(2,1)} %collective-permute-done, s32[1024]{0:T(1024)S(1)} %pad_clamp_fusion.1), kind=kCustom, calls=%fused_computation.3 | custom fusion | bytes 6291840 | tf_op jit(solution)/shard_map/gather | solution.py:78
  173.7 22.4 %all-gather.1 = f32[16,6,128]{2,1,0:T(8,128)S(1)} all-gather(f32[2,6,128]{2,1,0:T(8,128)S(1)} %pad_maximum_fusion), channel_id=3, replica_groups=mesh['row'=8,'chip'=16,'core'=2] {'row'}, dimensions={0}, use_global_device_ids=true | all-gather | bytes 55296 | tf_op jit(solution)/shard_map/all_gather | solution.py:64
  196.3 5.9 %convert_reduce_fusion.1 = f32[6,128,128]{2,1,0:T(8,128)S(1)} fusion(f32[8,6,128]{2,1,0:T(8,128)S(1)} %fusion.21, bf16[8,6,128,256]{3,2,1,0:T(8,128)(2,1)} %bitcast.64, bf16[6,8,256,128]{3,2,1,0:T(8,128)(2,1)} %bitcast.51, bf16[6,8,256,128]{3,2,1,0:T(8,128)(2,1)} %bitcast.52, pred[6,8,256]{2,1,0:T(8,128)(4,1)S(1)} %broadcast_in_dim.64), kind=kOutput, calls=%fused_computation.13 | convolution fusion | flops 407273472 | bytes 9867264 | tf_op jit(solution)/shard_map/gtmk,tgkc->gtmc/dot_general | solution.py:80
  202.2 0.8 fusion.17
  203.1 55.9 %all-gather.5.cloned.1.call-done = bf16[24576,128]{1,0:T(8,128)(2,1)} async-done(((bf16[768,128]{1,0:T(8,128)(2,1)}), bf16[24576,128]{1,0:T(8,128)(2,1)}) %all-gather.5.cloned.1.call-update) | async-done | bytes 6291472 | tf_op jit(solution)/shard_map/all_gather | solution.py:88
  259.0 5.5 %gather_fusion.4 = bf16[96,128,128]{2,1,0:T(8,128)(2,1)} fusion(bf16[192,128,128]{2,1,0:T(8,128)(2,1)} %bitcast.56, s32[1024]{0:T(1024)S(1)} %pad_clamp_fusion), kind=kCustom, calls=%fused_computation.4 | custom fusion | bytes 6291840 | tf_op jit(solution)/shard_map/gather | solution.py:75
  264.4 3.9 %convert_reduce_fusion = f32[6,128,128]{2,1,0:T(8,128)S(1)} fusion(f32[8,6,128]{2,1,0:T(8,128)S(1)} %fusion.21, bf16[8,6,128,256]{3,2,1,0:T(8,128)(2,1)} %bitcast.65, bf16[6,8,256,128]{3,2,1,0:T(8,128)(2,1)} %bitcast.53), kind=kOutput, calls=%fused_computation.11 | convolution fusion | flops 405700608 | bytes 6709248 | tf_op jit(solution)/shard_map/gtmk,tgkc->gtmc/dot_general | solution.py:80
  268.3 0.7 fusion.16
  (40 shorter events, 2.4 us)
Async XLA Ops:
  6.5 28.0 %copy-start = (bf16[768,1000]{0,1:T(8,128)(2,1)S(1)}, bf16[768,1000]{0,1:T(8,128)(2,1)}, u32[]{:S(2)}) copy-start(bf16[768,1000]{0,1:T(8,128)(2,1)} %param.6) | copy-start | bytes 4608004
  29.2 5.6 %copy-start.2 = (s32[768,50]{0,1:T(8,128)S(1)}, s32[768,50]{0,1:T(8,128)}, u32[]{:S(2)}) copy-start(s32[768,50]{0,1:T(8,128)} %param.9) | copy-start | bytes 460804
  29.2 78.6 %all-to-all-start.1 = ((bf16[32,128,768]{2,1,0:T(8,128)(2,1)}), bf16[32,128,768]{2,1,0:T(8,128)(2,1)}, u32[]{:S(2)}, u32[]{:S(2)}) async-start(bf16[32,128,768]{2,1,0:T(8,128)(2,1)} %gather_fusion), calls=%async_computation.1 | async-start | bytes 12582912 | tf_op jit(solution)/shard_map/all_to_all | solution.py:53
  110.1 15.0 %copy-start.3 = (f32[768]{0:T(1024)S(1)}, f32[768]{0:T(1024)}, u32[]{:S(2)}) copy-start(f32[768]{0:T(1024)} %param.7) | copy-start | bytes 9220
  110.1 50.0 %all-to-all-start.2 = ((bf16[16,768,128]{2,1,0:T(8,128)(2,1)}), bf16[16,768,128]{2,1,0:T(8,128)(2,1)}, u32[]{:S(2)}, u32[]{:S(2)}) async-start(bf16[16,768,128]{2,1,0:T(8,128)(2,1)} %stack.8), calls=%async_computation.2 | async-start | bytes 6291456 | tf_op jit(solution)/shard_map/all_to_all | solution.py:18
  117.4 12.7 %copy-start.1 = (bf16[768,768]{1,0:T(8,128)(2,1)S(1)}, bf16[768,768]{1,0:T(8,128)(2,1)}, u32[]{:S(2)}) copy-start(bf16[768,768]{1,0:T(8,128)(2,1)} %param.5) | copy-start | bytes 3538948
  117.5 78.8 %all-gather.7.cloned.1.call-start = ((), (), s32[]{:S(2)}) async-start(), calls=%async_computation.4 | async-start | bytes 3538944 | tf_op jit(solution)/shard_map/all_gather | solution.py:65
  133.8 125.2 %all-gather.5.cloned.1.call-start = ((), (), s32[]{:S(2)}) async-start(), calls=%async_computation.3 | async-start | bytes 6488064 | tf_op jit(solution)/shard_map/all_gather | solution.py:88
  160.2 9.0 %collective-permute-start = (bf16[96,128,128]{2,1,0:T(8,128)(2,1)}, bf16[96,128,128]{2,1,0:T(8,128)(2,1)}, u32[]{:S(2)}, u32[]{:S(2)}) collective-permute-start(bf16[96,128,128]{2,1,0:T(8,128)(2,1)} %bitcast.8), channel_id=1, source_target_pairs={{0,1},{1,0},{2,3},{3,2},{4,5},{5,4},{6,7},{7,6},{8,9},{9,8},{10,11... | collective-permute-start | bytes 9437192 | tf_op jit(solution)/shard_map/ppermute | solution.py:21
Sparse Core Ops, SparseCore 0:
  133.9 49.0 all-gather.6
  203.1 55.8 all-gather.4
